TPU v7x, 32 devices: a whole 2x2x4 slice. The times are simulated.
32 devices in a mesh: tx: 16 (over z, y, x), ty: 2 (over core).
Axes of the slice: x: 2, y: 2, z: 4, core: 2. Of those that a mesh axis runs over, the one named last changes fastest.
Arguments:
- pulses: bfloat16 [32, 2, 16384], P(('tx', 'ty')), may hold values from -6 to 6
- geometry: bfloat16 [5, 32], P(None, ('tx', 'ty')), as said below
- footprint: int32 [32, 8], P(('tx', 'ty')), may hold values from 0 to 15, as said below
- offsets: int32 [32, 16], P(None, 'tx'), may hold values from 0 to 15352
- image_in: float32 [2, 8192, 1024], P(None, 'tx', 'ty'), may hold values from -6 to 6
Outputs:
- image_out: float32 [2, 8192, 1024], P(None, 'tx', 'ty')
Inputs may be any that keep to these rules, and one draw needn't show every extreme that they name: `footprint`: each row is a run of 8 consecutive tile-row indices in ascending order. `geometry`: row 0 lies in 0.002 to 0.05, rows 1 and 4 in -pi to pi, row 2 in -0.05 to 0.05, row 3 in -0.02 to 0.02.
All inputs are finite; a program needn't handle non-finite values.
Results may differ from a plain program's by a relative error of at most 0.0027.
Values may be sent and summed in bfloat16 or wider, within the bound.
No kernel may reach another device: no remote copies, remote signals or barrier semaphores. Data moves between devices by JAX's collectives and lax.ppermute only.
A program may use at most 64 MiB of HBM per device.

v0:
```python
import math
import jax
import jax.numpy as jnp
from jax import lax
from jax.sharding import PartitionSpec as P

TAPS = 8


def make_taps(geometry, columns):
    rate = geometry[0].astype(jnp.float32)[:, None]
    shift = geometry[1].astype(jnp.float32)[:, None]
    ramp = geometry[2].astype(jnp.float32)[:, None]
    fraction = 0.5 + 0.45 * jnp.sin(rate * columns[None, :] + shift)
    places = jnp.arange(TAPS).astype(jnp.float32)
    spread = places[None, :, None] - 3.0 - fraction[:, None, :]
    angle_x = jnp.pi * spread
    kernel = jnp.sin(angle_x) / angle_x * (0.54 + 0.46 * jnp.cos(angle_x / 4.0))
    turning = ramp * columns[None, :]
    real_part = kernel * jnp.cos(turning)[:, None, :]
    imag_part = kernel * jnp.sin(turning)[:, None, :]
    return jnp.concatenate([real_part, imag_part], axis=1).astype(jnp.bfloat16)


def interpolate(windows, taps, width):
    real_sum = jnp.zeros((windows.shape[0], width), jnp.float32)
    imag_sum = jnp.zeros((windows.shape[0], width), jnp.float32)
    for k in range(TAPS):
        segment = windows[:, :, k : k + width].astype(jnp.float32)
        tap_real = taps[:, k].astype(jnp.float32)
        tap_imag = taps[:, TAPS + k].astype(jnp.float32)
        real_sum = real_sum + tap_real * segment[:, 0] - tap_imag * segment[:, 1]
        imag_sum = imag_sum + tap_real * segment[:, 1] + tap_imag * segment[:, 0]
    return jnp.concatenate([real_sum, imag_sum], axis=0).astype(jnp.bfloat16)


def phase_matrix(tilt, base_phase, rows):
    angles = (
        rows[:, None] * tilt.astype(jnp.float32)[None, :] + base_phase.astype(jnp.float32)[None, :]
    )
    cosine = jnp.cos(angles).astype(jnp.bfloat16)
    sine = jnp.sin(angles).astype(jnp.bfloat16)
    upper = jnp.concatenate([cosine, -sine], axis=1)
    lower = jnp.concatenate([sine, cosine], axis=1)
    return jnp.concatenate([upper, lower], axis=0)


def body(pulses, geometry, footprint, offsets, image_in):
    count_rows = lax.axis_size("tx")
    count_cols = lax.axis_size("ty")
    devices_all = count_rows * count_cols
    held = pulses.shape[0]
    tile_rows_n = image_in.shape[1]
    tile_cols_n = image_in.shape[2]
    length = tile_cols_n + TAPS
    wide_length = count_cols * tile_cols_n + TAPS
    myself = lax.axis_index("tx") * count_cols + lax.axis_index("ty")
    all_offsets = lax.all_gather(offsets, "tx", axis=1, tiled=True)
    mine = lax.dynamic_slice_in_dim(all_offsets, myself * held, held, 0)
    live = jnp.any(
        footprint[:, :, None] == jnp.arange(count_rows, dtype=jnp.int32)[None, None, :], axis=1
    )
    live_rows = live.T[:, None, :, None, None]

    def cut_window(signal, start):
        return lax.dynamic_slice_in_dim(signal, start, wide_length, 1)

    per_pulse = jax.vmap(cut_window, in_axes=(0, 0))
    per_row = jax.vmap(per_pulse, in_axes=(None, 0))
    row_windows = per_row(pulses, mine.T)
    pieces = [
        row_windows[:, :, :, j * tile_cols_n : j * tile_cols_n + length] for j in range(count_cols)
    ]
    windows = jnp.stack(pieces, axis=1)
    windows = jnp.where(live_rows, windows, jnp.zeros((), windows.dtype))
    windows = windows.reshape(devices_all, held, 2, length)
    slots = devices_all * held
    geo_send = jnp.broadcast_to(geometry.T[None], (devices_all, held, 5))
    got_windows, got_geo = (
        lax.all_to_all(windows, ("tx", "ty"), split_axis=0, concat_axis=0, tiled=True),
        lax.all_to_all(geo_send, ("tx", "ty"), split_axis=0, concat_axis=0, tiled=True),
    )
    got_geo = got_geo.reshape(slots, 5).T
    columns = (
        lax.axis_index("ty") * tile_cols_n + jnp.arange(tile_cols_n, dtype=jnp.int32)
    ).astype(jnp.float32)
    got_taps = make_taps(got_geo, columns)
    row_geo = got_geo[3:5]
    got_windows = got_windows.reshape(slots, 2, length)
    values = interpolate(got_windows, got_taps, tile_cols_n)
    rows = (lax.axis_index("tx") * tile_rows_n + jnp.arange(tile_rows_n, dtype=jnp.int32)).astype(
        jnp.float32
    )
    left = phase_matrix(row_geo[0], row_geo[1], rows)
    product = jnp.dot(left, values, preferred_element_type=jnp.float32).reshape(
        2, tile_rows_n, tile_cols_n
    )
    scale = 1.0 / math.sqrt(slots)
    return image_in + scale * product


def solution(mesh):
    in_specs = (
        P(("tx", "ty"), None, None),
        P(None, ("tx", "ty")),
        P(("tx", "ty"), None),
        P(None, "tx"),
        P(None, "tx", "ty"),
    )
    out_specs = P(None, "tx", "ty")
    return jax.shard_map(body, mesh=mesh, in_specs=in_specs, out_specs=out_specs, check_vma=False)
```

profile of v0, /device:TPU:0, one launch (start us, length us, event | category | flops | bytes accessed | tf_op | source)
XLA Modules:
  0.0 98.0 jit_solution(8685950877705287480)
XLA Ops:
  0.0 1.3 %broadcast_in_dim.21 = bf16[32,1,5]{2,1,0:T(2,128)(2,1)} broadcast(bf16[5]{0:T(256)(128)(2,1)} %bitcast.67), dimensions={2} | broadcast | bytes 330 | tf_op jit(solution)/shard_map/broadcast_in_dim | solution.py:78
  1.3 7.3 %all-to-all-start = ((bf16[32,1,5]{2,1,0:T(2,128)(2,1)}), bf16[32,1,5]{2,1,0:T(2,128)(2,1)S(1)}, u32[]{:S(2)}, u32[]{:S(2)}) async-start(bf16[32,1,5]{2,1,0:T(2,128)(2,1)} %broadcast_in_dim.21), calls=%async_computation | async-start | bytes 32768 | tf_op jit(solution)/shard_map/all_to_all | solution.py:81
  8.6 0.7 fusion.51
  9.5 40.9 %all-gather = s32[16,1,32]{2,1,0:T(1,128)S(1)} all-gather(s32[1,1,32]{2,1,0:T(1,128)} %bitcast.68), channel_id=1, replica_groups=mesh['tx'=16,'ty'=2] {'tx'}, dimensions={0}, use_global_device_ids=true | all-gather | bytes 2176 | tf_op jit(solution)/shard_map/all_gather | solution.py:58
  50.6 32.4 %while.1 = (s32[]{:T(128)}, bf16[1,2,16384]{2,1,0:T(2,128)(2,1)}, s32[16,3]{0,1:T(4,128)S(1)}, bf16[16,2,1032]{2,1,0:T(2,128)(2,1)S(1)}, s32[]{:T(128)}) while((s32[]{:T(128)}, bf16[1,2,16384]{2,1,0:T(2,128)(2,1)}, s32[16,3]{0,1:T(4,128)S(1)}, bf16[16,2,1032]{2,1,0:T(2,128)(2,1)S(1)}, s32[]{:T(128)}) %tuple.32), condition=%wide.while_cond, body=%wide.while_body.sunk | while | flops 2 | bytes 8849 | solution.py:66
  50.7 0.5 slice.359
  51.2 1.4 %dynamic-slice_dynamic-update-slice_fusion.2 = bf16[16,2,1032]{2,1,0:T(2,128)(2,1)S(1)} fusion(bf16[16,2,1032]{2,1,0:T(2,128)(2,1)S(1)} %get-tuple-element.76, s32[]{:T(128)S(6)} %copy.86, bf16[1,2,16384]{2,1,0:T(2,128)(2,1)} %get-tuple-element.79, s32[]{:T(128)} %bitcast.61), kind=kLoop, calls=%fused_computation.clone.1 | loop fusion | bytes 8744 | tf_op jit(solution)/shard_map/vmap(vmap())/gather
  52.7 0.5 slice.359
  53.2 1.4 %dynamic-slice_dynamic-update-slice_fusion.2 = bf16[16,2,1032]{2,1,0:T(2,128)(2,1)S(1)} fusion(bf16[16,2,1032]{2,1,0:T(2,128)(2,1)S(1)} %get-tuple-element.76, s32[]{:T(128)S(6)} %copy.86, bf16[1,2,16384]{2,1,0:T(2,128)(2,1)} %get-tuple-element.79, s32[]{:T(128)} %bitcast.61), kind=kLoop, calls=%fused_computation.clone.1 | loop fusion | bytes 8744 | tf_op jit(solution)/shard_map/vmap(vmap())/gather
  54.7 0.5 slice.359
  55.3 1.4 %dynamic-slice_dynamic-update-slice_fusion.2 = bf16[16,2,1032]{2,1,0:T(2,128)(2,1)S(1)} fusion(bf16[16,2,1032]{2,1,0:T(2,128)(2,1)S(1)} %get-tuple-element.76, s32[]{:T(128)S(6)} %copy.86, bf16[1,2,16384]{2,1,0:T(2,128)(2,1)} %get-tuple-element.79, s32[]{:T(128)} %bitcast.61), kind=kLoop, calls=%fused_computation.clone.1 | loop fusion | bytes 8744 | tf_op jit(solution)/shard_map/vmap(vmap())/gather
  56.7 0.5 slice.359
  57.3 1.4 %dynamic-slice_dynamic-update-slice_fusion.2 = bf16[16,2,1032]{2,1,0:T(2,128)(2,1)S(1)} fusion(bf16[16,2,1032]{2,1,0:T(2,128)(2,1)S(1)} %get-tuple-element.76, s32[]{:T(128)S(6)} %copy.86, bf16[1,2,16384]{2,1,0:T(2,128)(2,1)} %get-tuple-element.79, s32[]{:T(128)} %bitcast.61), kind=kLoop, calls=%fused_computation.clone.1 | loop fusion | bytes 8744 | tf_op jit(solution)/shard_map/vmap(vmap())/gather
  58.8 0.5 slice.359
  59.3 1.4 %dynamic-slice_dynamic-update-slice_fusion.2 = bf16[16,2,1032]{2,1,0:T(2,128)(2,1)S(1)} fusion(bf16[16,2,1032]{2,1,0:T(2,128)(2,1)S(1)} %get-tuple-element.76, s32[]{:T(128)S(6)} %copy.86, bf16[1,2,16384]{2,1,0:T(2,128)(2,1)} %get-tuple-element.79, s32[]{:T(128)} %bitcast.61), kind=kLoop, calls=%fused_computation.clone.1 | loop fusion | bytes 8744 | tf_op jit(solution)/shard_map/vmap(vmap())/gather
  60.8 0.5 slice.359
  61.3 1.4 %dynamic-slice_dynamic-update-slice_fusion.2 = bf16[16,2,1032]{2,1,0:T(2,128)(2,1)S(1)} fusion(bf16[16,2,1032]{2,1,0:T(2,128)(2,1)S(1)} %get-tuple-element.76, s32[]{:T(128)S(6)} %copy.86, bf16[1,2,16384]{2,1,0:T(2,128)(2,1)} %get-tuple-element.79, s32[]{:T(128)} %bitcast.61), kind=kLoop, calls=%fused_computation.clone.1 | loop fusion | bytes 8744 | tf_op jit(solution)/shard_map/vmap(vmap())/gather
  62.8 0.5 slice.359
  63.4 1.4 %dynamic-slice_dynamic-update-slice_fusion.2 = bf16[16,2,1032]{2,1,0:T(2,128)(2,1)S(1)} fusion(bf16[16,2,1032]{2,1,0:T(2,128)(2,1)S(1)} %get-tuple-element.76, s32[]{:T(128)S(6)} %copy.86, bf16[1,2,16384]{2,1,0:T(2,128)(2,1)} %get-tuple-element.79, s32[]{:T(128)} %bitcast.61), kind=kLoop, calls=%fused_computation.clone.1 | loop fusion | bytes 8744 | tf_op jit(solution)/shard_map/vmap(vmap())/gather
  64.8 0.5 slice.359
  65.4 1.4 %dynamic-slice_dynamic-update-slice_fusion.2 = bf16[16,2,1032]{2,1,0:T(2,128)(2,1)S(1)} fusion(bf16[16,2,1032]{2,1,0:T(2,128)(2,1)S(1)} %get-tuple-element.76, s32[]{:T(128)S(6)} %copy.86, bf16[1,2,16384]{2,1,0:T(2,128)(2,1)} %get-tuple-element.79, s32[]{:T(128)} %bitcast.61), kind=kLoop, calls=%fused_computation.clone.1 | loop fusion | bytes 8744 | tf_op jit(solution)/shard_map/vmap(vmap())/gather
  66.9 0.5 slice.359
  67.4 1.4 %dynamic-slice_dynamic-update-slice_fusion.2 = bf16[16,2,1032]{2,1,0:T(2,128)(2,1)S(1)} fusion(bf16[16,2,1032]{2,1,0:T(2,128)(2,1)S(1)} %get-tuple-element.76, s32[]{:T(128)S(6)} %copy.86, bf16[1,2,16384]{2,1,0:T(2,128)(2,1)} %get-tuple-element.79, s32[]{:T(128)} %bitcast.61), kind=kLoop, calls=%fused_computation.clone.1 | loop fusion | bytes 8744 | tf_op jit(solution)/shard_map/vmap(vmap())/gather
  68.9 0.5 slice.359
  69.4 1.4 %dynamic-slice_dynamic-update-slice_fusion.2 = bf16[16,2,1032]{2,1,0:T(2,128)(2,1)S(1)} fusion(bf16[16,2,1032]{2,1,0:T(2,128)(2,1)S(1)} %get-tuple-element.76, s32[]{:T(128)S(6)} %copy.86, bf16[1,2,16384]{2,1,0:T(2,128)(2,1)} %get-tuple-element.79, s32[]{:T(128)} %bitcast.61), kind=kLoop, calls=%fused_computation.clone.1 | loop fusion | bytes 8744 | tf_op jit(solution)/shard_map/vmap(vmap())/gather
  70.9 0.5 slice.359
  71.5 1.4 %dynamic-slice_dynamic-update-slice_fusion.2 = bf16[16,2,1032]{2,1,0:T(2,128)(2,1)S(1)} fusion(bf16[16,2,1032]{2,1,0:T(2,128)(2,1)S(1)} %get-tuple-element.76, s32[]{:T(128)S(6)} %copy.86, bf16[1,2,16384]{2,1,0:T(2,128)(2,1)} %get-tuple-element.79, s32[]{:T(128)} %bitcast.61), kind=kLoop, calls=%fused_computation.clone.1 | loop fusion | bytes 8744 | tf_op jit(solution)/shard_map/vmap(vmap())/gather
  72.9 0.5 slice.359
  73.5 1.4 %dynamic-slice_dynamic-update-slice_fusion.2 = bf16[16,2,1032]{2,1,0:T(2,128)(2,1)S(1)} fusion(bf16[16,2,1032]{2,1,0:T(2,128)(2,1)S(1)} %get-tuple-element.76, s32[]{:T(128)S(6)} %copy.86, bf16[1,2,16384]{2,1,0:T(2,128)(2,1)} %get-tuple-element.79, s32[]{:T(128)} %bitcast.61), kind=kLoop, calls=%fused_computation.clone.1 | loop fusion | bytes 8744 | tf_op jit(solution)/shard_map/vmap(vmap())/gather
  75.0 0.5 slice.359
  75.5 1.4 %dynamic-slice_dynamic-update-slice_fusion.2 = bf16[16,2,1032]{2,1,0:T(2,128)(2,1)S(1)} fusion(bf16[16,2,1032]{2,1,0:T(2,128)(2,1)S(1)} %get-tuple-element.76, s32[]{:T(128)S(6)} %copy.86, bf16[1,2,16384]{2,1,0:T(2,128)(2,1)} %get-tuple-element.79, s32[]{:T(128)} %bitcast.61), kind=kLoop, calls=%fused_computation.clone.1 | loop fusion | bytes 8744 | tf_op jit(solution)/shard_map/vmap(vmap())/gather
  77.0 0.5 slice.359
  77.5 1.4 %dynamic-slice_dynamic-update-slice_fusion.2 = bf16[16,2,1032]{2,1,0:T(2,128)(2,1)S(1)} fusion(bf16[16,2,1032]{2,1,0:T(2,128)(2,1)S(1)} %get-tuple-element.76, s32[]{:T(128)S(6)} %copy.86, bf16[1,2,16384]{2,1,0:T(2,128)(2,1)} %get-tuple-element.79, s32[]{:T(128)} %bitcast.61), kind=kLoop, calls=%fused_computation.clone.1 | loop fusion | bytes 8744 | tf_op jit(solution)/shard_map/vmap(vmap())/gather
  79.0 0.5 slice.359
  79.6 1.4 %dynamic-slice_dynamic-update-slice_fusion.2 = bf16[16,2,1032]{2,1,0:T(2,128)(2,1)S(1)} fusion(bf16[16,2,1032]{2,1,0:T(2,128)(2,1)S(1)} %get-tuple-element.76, s32[]{:T(128)S(6)} %copy.86, bf16[1,2,16384]{2,1,0:T(2,128)(2,1)} %get-tuple-element.79, s32[]{:T(128)} %bitcast.61), kind=kLoop, calls=%fused_computation.clone.1 | loop fusion | bytes 8744 | tf_op jit(solution)/shard_map/vmap(vmap())/gather
  81.0 0.5 slice.359
  81.6 1.4 %dynamic-slice_dynamic-update-slice_fusion.2 = bf16[16,2,1032]{2,1,0:T(2,128)(2,1)S(1)} fusion(bf16[16,2,1032]{2,1,0:T(2,128)(2,1)S(1)} %get-tuple-element.76, s32[]{:T(128)S(6)} %copy.86, bf16[1,2,16384]{2,1,0:T(2,128)(2,1)} %get-tuple-element.79, s32[]{:T(128)} %bitcast.61), kind=kLoop, calls=%fused_computation.clone.1 | loop fusion | bytes 8744 | tf_op jit(solution)/shard_map/vmap(vmap())/gather
  83.3 0.8 fusion.11
  84.1 2.6 %all-to-all-start.1 = ((bf16[32,1,2,520]{3,2,1,0:T(2,128)(2,1)}), bf16[32,1,2,520]{3,2,1,0:T(2,128)(2,1)S(1)}, u32[]{:S(2)}, u32[]{:S(2)}) async-start(bf16[32,1,2,520]{3,2,1,0:T(2,128)(2,1)} %fusion.11), calls=%async_computation.1 | async-start | bytes 163840 | tf_op jit(solution)/shard_map/all_to_all | solution.py:80
  86.7 0.3 sine_convert_fusion
  87.1 0.5 multiply_cosine_fusion
  87.6 3.8 %multiply_convert_fusion.1 = (bf16[32,8,512]{2,0,1:T(8,128)(2,1)S(1)}, bf16[32,8,512]{2,0,1:T(8,128)(2,1)S(1)}) fusion(f32[32,512]{1,0:T(8,128)S(1)} %get-tuple-element.35, f32[32,512]{1,0:T(8,128)S(1)} %get-tuple-element.37, f32[8]{0:T(128)S(1)} %convert_add_fusion, f32[32,512]{1,0:T(8,128)S(1)} %get-tuple-element.36), kind=kLoop, calls=%fused_computation.11 | loop fusion | flops 1441792 | bytes 720928 | tf_op jit(solution)/shard_map/convert.7
  91.4 0.3 fusion.53
  91.7 2.6 %all-to-all-done.1 = bf16[32,1,2,520]{3,2,1,0:T(2,128)(2,1)S(1)} async-done(((bf16[32,1,2,520]{3,2,1,0:T(2,128)(2,1)}), bf16[32,1,2,520]{3,2,1,0:T(2,128)(2,1)S(1)}, u32[]{:S(2)}, u32[]{:S(2)}) %all-to-all-start.1) | async-done | bytes 66592 | tf_op jit(solution)/shard_map/all_to_all | solution.py:80
  94.3 0.2 slice_convert_fusion.7
  94.8 0.5 convolution_multiply_fusion
  95.3 0.9 copy-done
  96.2 1.8 %add.204 = f32[2,512,512]{2,1,0:T(8,128)} add(f32[2,512,512]{2,1,0:T(8,128)S(1)} %copy-done, f32[2,512,512]{2,1,0:T(8,128)S(1)} %bitcast.62) | non-fusion elementwise | flops 524288 | bytes 6291456 | tf_op jit(solution)/shard_map/add | solution.py:99
  (35 shorter events, 2.2 us)
Async XLA Ops:
  1.3 82.8 %all-to-all-start = ((bf16[32,1,5]{2,1,0:T(2,128)(2,1)}), bf16[32,1,5]{2,1,0:T(2,128)(2,1)S(1)}, u32[]{:S(2)}, u32[]{:S(2)}) async-start(bf16[32,1,5]{2,1,0:T(2,128)(2,1)} %broadcast_in_dim.21), calls=%async_computation | async-start | bytes 32768 | tf_op jit(solution)/shard_map/all_to_all | solution.py:81
  84.1 10.2 %all-to-all-start.1 = ((bf16[32,1,2,520]{3,2,1,0:T(2,128)(2,1)}), bf16[32,1,2,520]{3,2,1,0:T(2,128)(2,1)S(1)}, u32[]{:S(2)}, u32[]{:S(2)}) async-start(bf16[32,1,2,520]{3,2,1,0:T(2,128)(2,1)} %fusion.11), calls=%async_computation.1 | async-start | bytes 163840 | tf_op jit(solution)/shard_map/all_to_all | solution.py:80
  94.6 1.6 %copy-start = (f32[2,512,512]{2,1,0:T(8,128)S(1)}, f32[2,512,512]{2,1,0:T(8,128)}, u32[]{:S(2)}) copy-start(f32[2,512,512]{2,1,0:T(8,128)} %param.9) | copy-start | bytes 6291460
where the time goes:
time: 99 us; the launch traced here: 98 us
  blocking collectives  40.9 us (41%)
  local copies, waits for them, and re-layouts  35.1 us (35%)
  starting transfers between devices  9.87 us (10%)
  other arithmetic  9.01 us (9%)
  waiting for transfers between devices  2.57 us (3%)
    all_gather x1, blocking collectives, body(): all_offsets = lax.all_gather(offsets, 'tx', axis=1, tiled=True)  40.9 us
    gather x48, local copies, waits for them, and re-layouts  32.4 us
    all_to_all x1, starting transfers between devices, body(): lax.all_to_all(geo_send, ('tx', 'ty'), split_axis=0, concat_axis=0, tiled...  7.3 us
    another operation x3, other arithmetic  4.1 us
    all_to_all x1, starting transfers between devices, body(): lax.all_to_all(windows, ('tx', 'ty'), split_axis=0, concat_axis=0, tiled=...  2.57 us
    all_to_all x1, waiting for transfers between devices, body(): lax.all_to_all(windows, ('tx', 'ty'), split_axis=0, concat_axis=0, tiled=...  2.56 us
  transfers between devices with their start and end apart: 2, of which 1 were waited for; matrix products, arithmetic and copies ran while one was open for 40% of the time, Pallas kernels for 0%

commit v1 on v0

--- a/solution.py
+++ b/solution.py
@@ -55,7 +55,16 @@
     length = tile_cols_n + TAPS
     wide_length = count_cols * tile_cols_n + TAPS
     myself = lax.axis_index("tx") * count_cols + lax.axis_index("ty")
-    all_offsets = lax.all_gather(offsets, "tx", axis=1, tiled=True)
+    ways = lax.axis_size("tx")
+    up = [(d, (d + 1) % ways) for d in range(ways)]
+    down = [(d, (d - 1) % ways) for d in range(ways)]
+    earlier, later = ([offsets], [offsets])
+    for _ in range(ways // 2):
+        earlier.append(lax.ppermute(earlier[-1], "tx", up))
+    for _ in range((ways - 1) // 2):
+        later.append(lax.ppermute(later[-1], "tx", down))
+    line = jnp.concatenate([*earlier[::-1], *later[1:]], axis=1)
+    all_offsets = jnp.roll(line, (lax.axis_index("tx") - ways // 2) * offsets.shape[1], axis=1)
     mine = lax.dynamic_slice_in_dim(all_offsets, myself * held, held, 0)
     live = jnp.any(
         footprint[:, :, None] == jnp.arange(count_rows, dtype=jnp.int32)[None, None, :], axis=1

time: 99 us -> 115 us (1.16)
  blocking collectives: 40.9 us -> 0 us
  starting transfers between devices: 9.87 us -> 45.9 us
  waiting for transfers between devices: 2.57 us -> 21.7 us
  local copies, waits for them, and re-layouts: 35.1 us -> 36.4 us
    all_gather x1 -> x0, blocking collectives: 40.9 us -> none  [body(): all_offsets = lax.all_gather(offsets, 'tx', axis=1, tiled=True)]
    ppermute x0 -> x15, starting transfers between devices: none -> 40.8 us  [the longest x7 36.1 us: body(): later.append(lax.ppermute(later[-1], 'tx', down))]
    ppermute x0 -> x15, waiting for transfers between devices: none -> 14.4 us  [the longest x8 14.4 us: body(): earlier.append(lax.ppermute(earlier[-1], 'tx', up))]
    all_to_all x1, starting transfers between devices: 7.3 us -> 2.54 us  [body(): lax.all_to_all(geo_send, ('tx', 'ty'), split_axis=0, concat_axis=0, tiled...]
    all_to_all x1, waiting for transfers between devices: 2.56 us -> 7.3 us  [body(): lax.all_to_all(windows, ('tx', 'ty'), split_axis=0, concat_axis=0, tiled=...]
    concatenate x0 -> x1, local copies, waits for them, and re-layouts: none -> 1.39 us  [body(): jnp.roll(line, (lax.axis_index('tx') - ways // 2) * offsets.shape[1], axi...]
  transfers between devices with their start and end apart: 2 -> 17, of which waited for: 1 -> 7; matrix products, arithmetic and copies ran while one was open for 40% -> 6% of each run, Pallas kernels for 0% -> 0%
where the time goes in v1:
time: 115 us; the launch traced here: 114 us
  starting transfers between devices  45.9 us (40%)
  local copies, waits for them, and re-layouts  36.4 us (32%)
  waiting for transfers between devices  21.7 us (19%)
  other arithmetic  8.94 us (8%)
    ppermute x7, starting transfers between devices, body(): later.append(lax.ppermute(later[-1], 'tx', down))  36.1 us
    gather x48, local copies, waits for them, and re-layouts  32.2 us
    ppermute x8, waiting for transfers between devices, body(): earlier.append(lax.ppermute(earlier[-1], 'tx', up))  14.4 us
    all_to_all x1, waiting for transfers between devices, body(): lax.all_to_all(windows, ('tx', 'ty'), split_axis=0, concat_axis=0, tiled=...  7.3 us
    ppermute x8, starting transfers between devices, body(): earlier.append(lax.ppermute(earlier[-1], 'tx', up))  4.7 us
    another operation x3, other arithmetic  4.1 us
    all_to_all x1, starting transfers between devices, body(): lax.all_to_all(windows, ('tx', 'ty'), split_axis=0, concat_axis=0, tiled=...  2.57 us
    all_to_all x1, starting transfers between devices, body(): lax.all_to_all(geo_send, ('tx', 'ty'), split_axis=0, concat_axis=0, tiled...  2.54 us
  transfers between devices with their start and end apart: 17, of which 7 were waited for; matrix products, arithmetic and copies ran while one was open for 6% of the time, Pallas kernels for 0%

profile of v1, /device:TPU:0, one launch (start us, length us, event | category | flops | bytes accessed | tf_op | source)
XLA Modules:
  0.0 113.6 jit_solution(15495692862578484601)
XLA Ops:
  0.0 2.9 %collective-permute-start = (s32[32,1]{0,1:T(1,128)}, s32[32,1]{0,1:T(1,128)S(1)}, u32[]{:S(2)}, u32[]{:S(2)}) collective-permute-start(s32[32,1]{0,1:T(1,128)} %param.8), channel_id=1, source_target_pairs={{0,2},{2,4},{4,6},{6,8},{8,10},{10,12},{12,14},{14,16},{16,18},{18... | collective-permute-start | bytes 392 | tf_op jit(solution)/shard_map/ppermute | solution.py:63
  2.9 4.0 %collective-permute-start.8 = (s32[32,1]{0,1:T(1,128)}, s32[32,1]{0,1:T(1,128)S(1)}, u32[]{:S(2)}, u32[]{:S(2)}) collective-permute-start(s32[32,1]{0,1:T(1,128)} %param.8), channel_id=1, source_target_pairs={{0,30},{2,0},{4,2},{6,4},{8,6},{10,8},{12,10},{14,12},{16,14},{18,... | collective-permute-start | bytes 392 | tf_op jit(solution)/shard_map/ppermute | solution.py:65
  6.9 1.3 %broadcast_in_dim.21 = bf16[32,1,5]{2,1,0:T(2,128)(2,1)} broadcast(bf16[5]{0:T(256)(128)(2,1)} %bitcast.68), dimensions={2} | broadcast | bytes 330 | tf_op jit(solution)/shard_map/broadcast_in_dim | solution.py:87
  8.2 2.5 %all-to-all-start = ((bf16[32,1,5]{2,1,0:T(2,128)(2,1)}), bf16[32,1,5]{2,1,0:T(2,128)(2,1)S(1)}, u32[]{:S(2)}, u32[]{:S(2)}) async-start(bf16[32,1,5]{2,1,0:T(2,128)(2,1)} %broadcast_in_dim.21), calls=%async_computation | async-start | bytes 32768 | tf_op jit(solution)/shard_map/all_to_all | solution.py:90
  10.8 0.7 fusion.51
  11.8 1.7 %collective-permute-start.1 = (s32[32,1]{0,1:T(1,128)S(1)}, s32[32,1]{0,1:T(1,128)S(1)}, u32[]{:S(2)}, u32[]{:S(2)}) collective-permute-start(s32[32,1]{0,1:T(1,128)S(1)} %collective-permute-done), channel_id=1, source_target_pairs={{0,2},{2,4},{4,6},{6,8},{8,10},{10,12},{12,14},{14,16},{16,18},{18... | collective-permute-start | bytes 392 | tf_op jit(solution)/shard_map/ppermute | solution.py:63
  13.5 4.0 %collective-permute-start.9 = (s32[32,1]{0,1:T(1,128)S(1)}, s32[32,1]{0,1:T(1,128)S(1)}, u32[]{:S(2)}, u32[]{:S(2)}) collective-permute-start(s32[32,1]{0,1:T(1,128)S(1)} %collective-permute-done.8), channel_id=1, source_target_pairs={{0,30},{2,0},{4,2},{6,4},{8,6},{10,8},{12,10},{14,12},{16,14},{18,... | collective-permute-start | bytes 392 | tf_op jit(solution)/shard_map/ppermute | solution.py:65
  17.5 1.5 %collective-permute-done.1 = s32[32,1]{0,1:T(1,128)S(1)} collective-permute-done((s32[32,1]{0,1:T(1,128)S(1)}, s32[32,1]{0,1:T(1,128)S(1)}, u32[]{:S(2)}, u32[]{:S(2)}) %collective-permute-start.1) | collective-permute-done | bytes 160 | tf_op jit(solution)/shard_map/ppermute | solution.py:63
  19.0 5.6 %collective-permute-start.10 = (s32[32,1]{0,1:T(1,128)S(1)}, s32[32,1]{0,1:T(1,128)S(1)}, u32[]{:S(2)}, u32[]{:S(2)}) collective-permute-start(s32[32,1]{0,1:T(1,128)S(1)} %collective-permute-done.9), channel_id=1, source_target_pairs={{0,30},{2,0},{4,2},{6,4},{8,6},{10,8},{12,10},{14,12},{16,14},{18,... | collective-permute-start | bytes 392 | tf_op jit(solution)/shard_map/ppermute | solution.py:65
  24.6 1.5 %collective-permute-done.2 = s32[32,1]{0,1:T(1,128)S(1)} collective-permute-done((s32[32,1]{0,1:T(1,128)S(1)}, s32[32,1]{0,1:T(1,128)S(1)}, u32[]{:S(2)}, u32[]{:S(2)}) %collective-permute-start.2) | collective-permute-done | bytes 160 | tf_op jit(solution)/shard_map/ppermute | solution.py:63
  26.1 5.6 %collective-permute-start.11 = (s32[32,1]{0,1:T(1,128)S(1)}, s32[32,1]{0,1:T(1,128)S(1)}, u32[]{:S(2)}, u32[]{:S(2)}) collective-permute-start(s32[32,1]{0,1:T(1,128)S(1)} %collective-permute-done.10), channel_id=1, source_target_pairs={{0,30},{2,0},{4,2},{6,4},{8,6},{10,8},{12,10},{14,12},{16,14},{18,... | collective-permute-start | bytes 392 | tf_op jit(solution)/shard_map/ppermute | solution.py:65
  31.7 1.5 %collective-permute-done.3 = s32[32,1]{0,1:T(1,128)S(1)} collective-permute-done((s32[32,1]{0,1:T(1,128)S(1)}, s32[32,1]{0,1:T(1,128)S(1)}, u32[]{:S(2)}, u32[]{:S(2)}) %collective-permute-start.3) | collective-permute-done | bytes 160 | tf_op jit(solution)/shard_map/ppermute | solution.py:63
  33.2 5.6 %collective-permute-start.12 = (s32[32,1]{0,1:T(1,128)S(1)}, s32[32,1]{0,1:T(1,128)S(1)}, u32[]{:S(2)}, u32[]{:S(2)}) collective-permute-start(s32[32,1]{0,1:T(1,128)S(1)} %collective-permute-done.11), channel_id=1, source_target_pairs={{0,30},{2,0},{4,2},{6,4},{8,6},{10,8},{12,10},{14,12},{16,14},{18,... | collective-permute-start | bytes 392 | tf_op jit(solution)/shard_map/ppermute | solution.py:65
  39.0 0.5 multiply_cosine_fusion
  39.5 3.8 %multiply_convert_fusion.1 = (bf16[32,8,512]{2,0,1:T(8,128)(2,1)S(1)}, bf16[32,8,512]{2,0,1:T(8,128)(2,1)S(1)}) fusion(f32[32,512]{1,0:T(8,128)S(1)} %get-tuple-element.35, f32[32,512]{1,0:T(8,128)S(1)} %get-tuple-element.37, f32[8]{0:T(128)S(1)} %convert_add_fusion, f32[32,512]{1,0:T(8,128)S(1)} %get-tuple-element.36), kind=kLoop, calls=%fused_computation.11 | loop fusion | flops 1441792 | bytes 720928 | tf_op jit(solution)/shard_map/convert.7
  43.4 5.6 %collective-permute-start.13 = (s32[32,1]{0,1:T(1,128)S(1)}, s32[32,1]{0,1:T(1,128)S(1)}, u32[]{:S(2)}, u32[]{:S(2)}) collective-permute-start(s32[32,1]{0,1:T(1,128)S(1)} %collective-permute-done.12), channel_id=1, source_target_pairs={{0,30},{2,0},{4,2},{6,4},{8,6},{10,8},{12,10},{14,12},{16,14},{18,... | collective-permute-start | bytes 392 | tf_op jit(solution)/shard_map/ppermute | solution.py:65
  49.0 1.5 %collective-permute-done.5 = s32[32,1]{0,1:T(1,128)S(1)} collective-permute-done((s32[32,1]{0,1:T(1,128)S(1)}, s32[32,1]{0,1:T(1,128)S(1)}, u32[]{:S(2)}, u32[]{:S(2)}) %collective-permute-start.5) | collective-permute-done | bytes 160 | tf_op jit(solution)/shard_map/ppermute | solution.py:63
  50.5 5.6 %collective-permute-start.14 = (s32[32,1]{0,1:T(1,128)S(1)}, s32[32,1]{0,1:T(1,128)S(1)}, u32[]{:S(2)}, u32[]{:S(2)}) collective-permute-start(s32[32,1]{0,1:T(1,128)S(1)} %collective-permute-done.13), channel_id=1, source_target_pairs={{0,30},{2,0},{4,2},{6,4},{8,6},{10,8},{12,10},{14,12},{16,14},{18,... | collective-permute-start | bytes 392 | tf_op jit(solution)/shard_map/ppermute | solution.py:65
  56.1 1.5 %collective-permute-done.6 = s32[32,1]{0,1:T(1,128)S(1)} collective-permute-done((s32[32,1]{0,1:T(1,128)S(1)}, s32[32,1]{0,1:T(1,128)S(1)}, u32[]{:S(2)}, u32[]{:S(2)}) %collective-permute-start.6) | collective-permute-done | bytes 160 | tf_op jit(solution)/shard_map/ppermute | solution.py:63
  58.0 6.8 %collective-permute-done.7 = s32[32,1]{0,1:T(1,128)S(1)} collective-permute-done((s32[32,1]{0,1:T(1,128)S(1)}, s32[32,1]{0,1:T(1,128)S(1)}, u32[]{:S(2)}, u32[]{:S(2)}) %collective-permute-start.7) | collective-permute-done | bytes 160 | tf_op jit(solution)/shard_map/ppermute | solution.py:63
  64.8 1.4 %concatenate.29 = s32[32,32]{0,1:T(8,128)S(1)} concatenate(s32[32,1]{0,1:T(1,128)S(1)} %collective-permute-done.7, s32[32,1]{0,1:T(1,128)S(1)} %collective-permute-done.6, s32[32,1]{0,1:T(1,128)S(1)} %collective-permute-done.5, s32[32,1]{0,1:T(1,128)S(1)} %collective-permute-done.4, s32[32,1]{0,1:T(1,128)S(1)} %collective-permute-done.3, s32[32,1]{0,1:T(1,128)S(1)} %collective-permute-done.2, ...), dimensions={1} | concatenate | bytes 8192 | tf_op jit(solution)/shard_map/jit(_roll_dynamic)/concatenate | solution.py:67
  66.4 32.2 %while.1 = (s32[]{:T(128)}, bf16[1,2,16384]{2,1,0:T(2,128)(2,1)}, s32[16,3]{0,1:T(4,128)S(1)}, bf16[16,2,1032]{2,1,0:T(2,128)(2,1)S(1)}, s32[]{:T(128)}) while((s32[]{:T(128)}, bf16[1,2,16384]{2,1,0:T(2,128)(2,1)}, s32[16,3]{0,1:T(4,128)S(1)}, bf16[16,2,1032]{2,1,0:T(2,128)(2,1)S(1)}, s32[]{:T(128)}) %tuple.32), condition=%wide.while_cond, body=%wide.while_body.sunk | while | flops 2 | bytes 8849 | solution.py:75
  67.0 1.4 %dynamic-slice_dynamic-update-slice_fusion.2 = bf16[16,2,1032]{2,1,0:T(2,128)(2,1)S(1)} fusion(bf16[16,2,1032]{2,1,0:T(2,128)(2,1)S(1)} %get-tuple-element.76, s32[]{:T(128)S(6)} %copy.78, bf16[1,2,16384]{2,1,0:T(2,128)(2,1)} %get-tuple-element.79, s32[]{:T(128)} %bitcast.62), kind=kLoop, calls=%fused_computation.clone.1 | loop fusion | bytes 8744 | tf_op jit(solution)/shard_map/vmap(vmap())/gather
  68.5 0.5 slice.359
  69.0 1.4 %dynamic-slice_dynamic-update-slice_fusion.2 = bf16[16,2,1032]{2,1,0:T(2,128)(2,1)S(1)} fusion(bf16[16,2,1032]{2,1,0:T(2,128)(2,1)S(1)} %get-tuple-element.76, s32[]{:T(128)S(6)} %copy.78, bf16[1,2,16384]{2,1,0:T(2,128)(2,1)} %get-tuple-element.79, s32[]{:T(128)} %bitcast.62), kind=kLoop, calls=%fused_computation.clone.1 | loop fusion | bytes 8744 | tf_op jit(solution)/shard_map/vmap(vmap())/gather
  70.5 0.5 slice.359
  71.0 1.4 %dynamic-slice_dynamic-update-slice_fusion.2 = bf16[16,2,1032]{2,1,0:T(2,128)(2,1)S(1)} fusion(bf16[16,2,1032]{2,1,0:T(2,128)(2,1)S(1)} %get-tuple-element.76, s32[]{:T(128)S(6)} %copy.78, bf16[1,2,16384]{2,1,0:T(2,128)(2,1)} %get-tuple-element.79, s32[]{:T(128)} %bitcast.62), kind=kLoop, calls=%fused_computation.clone.1 | loop fusion | bytes 8744 | tf_op jit(solution)/shard_map/vmap(vmap())/gather
  72.5 0.5 slice.359
  73.0 1.4 %dynamic-slice_dynamic-update-slice_fusion.2 = bf16[16,2,1032]{2,1,0:T(2,128)(2,1)S(1)} fusion(bf16[16,2,1032]{2,1,0:T(2,128)(2,1)S(1)} %get-tuple-element.76, s32[]{:T(128)S(6)} %copy.78, bf16[1,2,16384]{2,1,0:T(2,128)(2,1)} %get-tuple-element.79, s32[]{:T(128)} %bitcast.62), kind=kLoop, calls=%fused_computation.clone.1 | loop fusion | bytes 8744 | tf_op jit(solution)/shard_map/vmap(vmap())/gather
  74.5 0.5 slice.359
  75.0 1.4 %dynamic-slice_dynamic-update-slice_fusion.2 = bf16[16,2,1032]{2,1,0:T(2,128)(2,1)S(1)} fusion(bf16[16,2,1032]{2,1,0:T(2,128)(2,1)S(1)} %get-tuple-element.76, s32[]{:T(128)S(6)} %copy.78, bf16[1,2,16384]{2,1,0:T(2,128)(2,1)} %get-tuple-element.79, s32[]{:T(128)} %bitcast.62), kind=kLoop, calls=%fused_computation.clone.1 | loop fusion | bytes 8744 | tf_op jit(solution)/shard_map/vmap(vmap())/gather
  76.5 0.5 slice.359
  77.0 1.4 %dynamic-slice_dynamic-update-slice_fusion.2 = bf16[16,2,1032]{2,1,0:T(2,128)(2,1)S(1)} fusion(bf16[16,2,1032]{2,1,0:T(2,128)(2,1)S(1)} %get-tuple-element.76, s32[]{:T(128)S(6)} %copy.78, bf16[1,2,16384]{2,1,0:T(2,128)(2,1)} %get-tuple-element.79, s32[]{:T(128)} %bitcast.62), kind=kLoop, calls=%fused_computation.clone.1 | loop fusion | bytes 8744 | tf_op jit(solution)/shard_map/vmap(vmap())/gather
  79.0 1.4 %dynamic-slice_dynamic-update-slice_fusion.2 = bf16[16,2,1032]{2,1,0:T(2,128)(2,1)S(1)} fusion(bf16[16,2,1032]{2,1,0:T(2,128)(2,1)S(1)} %get-tuple-element.76, s32[]{:T(128)S(6)} %copy.78, bf16[1,2,16384]{2,1,0:T(2,128)(2,1)} %get-tuple-element.79, s32[]{:T(128)} %bitcast.62), kind=kLoop, calls=%fused_computation.clone.1 | loop fusion | bytes 8744 | tf_op jit(solution)/shard_map/vmap(vmap())/gather
  81.1 1.4 %dynamic-slice_dynamic-update-slice_fusion.2 = bf16[16,2,1032]{2,1,0:T(2,128)(2,1)S(1)} fusion(bf16[16,2,1032]{2,1,0:T(2,128)(2,1)S(1)} %get-tuple-element.76, s32[]{:T(128)S(6)} %copy.78, bf16[1,2,16384]{2,1,0:T(2,128)(2,1)} %get-tuple-element.79, s32[]{:T(128)} %bitcast.62), kind=kLoop, calls=%fused_computation.clone.1 | loop fusion | bytes 8744 | tf_op jit(solution)/shard_map/vmap(vmap())/gather
  83.1 1.4 %dynamic-slice_dynamic-update-slice_fusion.2 = bf16[16,2,1032]{2,1,0:T(2,128)(2,1)S(1)} fusion(bf16[16,2,1032]{2,1,0:T(2,128)(2,1)S(1)} %get-tuple-element.76, s32[]{:T(128)S(6)} %copy.78, bf16[1,2,16384]{2,1,0:T(2,128)(2,1)} %get-tuple-element.79, s32[]{:T(128)} %bitcast.62), kind=kLoop, calls=%fused_computation.clone.1 | loop fusion | bytes 8744 | tf_op jit(solution)/shard_map/vmap(vmap())/gather
  85.1 1.4 %dynamic-slice_dynamic-update-slice_fusion.2 = bf16[16,2,1032]{2,1,0:T(2,128)(2,1)S(1)} fusion(bf16[16,2,1032]{2,1,0:T(2,128)(2,1)S(1)} %get-tuple-element.76, s32[]{:T(128)S(6)} %copy.78, bf16[1,2,16384]{2,1,0:T(2,128)(2,1)} %get-tuple-element.79, s32[]{:T(128)} %bitcast.62), kind=kLoop, calls=%fused_computation.clone.1 | loop fusion | bytes 8744 | tf_op jit(solution)/shard_map/vmap(vmap())/gather
  87.1 1.4 %dynamic-slice_dynamic-update-slice_fusion.2 = bf16[16,2,1032]{2,1,0:T(2,128)(2,1)S(1)} fusion(bf16[16,2,1032]{2,1,0:T(2,128)(2,1)S(1)} %get-tuple-element.76, s32[]{:T(128)S(6)} %copy.78, bf16[1,2,16384]{2,1,0:T(2,128)(2,1)} %get-tuple-element.79, s32[]{:T(128)} %bitcast.62), kind=kLoop, calls=%fused_computation.clone.1 | loop fusion | bytes 8744 | tf_op jit(solution)/shard_map/vmap(vmap())/gather
  89.1 1.4 %dynamic-slice_dynamic-update-slice_fusion.2 = bf16[16,2,1032]{2,1,0:T(2,128)(2,1)S(1)} fusion(bf16[16,2,1032]{2,1,0:T(2,128)(2,1)S(1)} %get-tuple-element.76, s32[]{:T(128)S(6)} %copy.78, bf16[1,2,16384]{2,1,0:T(2,128)(2,1)} %get-tuple-element.79, s32[]{:T(128)} %bitcast.62), kind=kLoop, calls=%fused_computation.clone.1 | loop fusion | bytes 8744 | tf_op jit(solution)/shard_map/vmap(vmap())/gather
  91.1 1.4 %dynamic-slice_dynamic-update-slice_fusion.2 = bf16[16,2,1032]{2,1,0:T(2,128)(2,1)S(1)} fusion(bf16[16,2,1032]{2,1,0:T(2,128)(2,1)S(1)} %get-tuple-element.76, s32[]{:T(128)S(6)} %copy.78, bf16[1,2,16384]{2,1,0:T(2,128)(2,1)} %get-tuple-element.79, s32[]{:T(128)} %bitcast.62), kind=kLoop, calls=%fused_computation.clone.1 | loop fusion | bytes 8744 | tf_op jit(solution)/shard_map/vmap(vmap())/gather
  93.1 1.4 %dynamic-slice_dynamic-update-slice_fusion.2 = bf16[16,2,1032]{2,1,0:T(2,128)(2,1)S(1)} fusion(bf16[16,2,1032]{2,1,0:T(2,128)(2,1)S(1)} %get-tuple-element.76, s32[]{:T(128)S(6)} %copy.78, bf16[1,2,16384]{2,1,0:T(2,128)(2,1)} %get-tuple-element.79, s32[]{:T(128)} %bitcast.62), kind=kLoop, calls=%fused_computation.clone.1 | loop fusion | bytes 8744 | tf_op jit(solution)/shard_map/vmap(vmap())/gather
  95.1 1.4 %dynamic-slice_dynamic-update-slice_fusion.2 = bf16[16,2,1032]{2,1,0:T(2,128)(2,1)S(1)} fusion(bf16[16,2,1032]{2,1,0:T(2,128)(2,1)S(1)} %get-tuple-element.76, s32[]{:T(128)S(6)} %copy.78, bf16[1,2,16384]{2,1,0:T(2,128)(2,1)} %get-tuple-element.79, s32[]{:T(128)} %bitcast.62), kind=kLoop, calls=%fused_computation.clone.1 | loop fusion | bytes 8744 | tf_op jit(solution)/shard_map/vmap(vmap())/gather
  97.2 1.4 %dynamic-slice_dynamic-update-slice_fusion.2 = bf16[16,2,1032]{2,1,0:T(2,128)(2,1)S(1)} fusion(bf16[16,2,1032]{2,1,0:T(2,128)(2,1)S(1)} %get-tuple-element.76, s32[]{:T(128)S(6)} %copy.78, bf16[1,2,16384]{2,1,0:T(2,128)(2,1)} %get-tuple-element.79, s32[]{:T(128)} %bitcast.62), kind=kLoop, calls=%fused_computation.clone.1 | loop fusion | bytes 8744 | tf_op jit(solution)/shard_map/vmap(vmap())/gather
  98.8 0.8 fusion.11
  99.6 2.6 %all-to-all-start.1 = ((bf16[32,1,2,520]{3,2,1,0:T(2,128)(2,1)}), bf16[32,1,2,520]{3,2,1,0:T(2,128)(2,1)S(1)}, u32[]{:S(2)}, u32[]{:S(2)}) async-start(bf16[32,1,2,520]{3,2,1,0:T(2,128)(2,1)} %fusion.11), calls=%async_computation.1 | async-start | bytes 163840 | tf_op jit(solution)/shard_map/all_to_all | solution.py:89
  102.5 7.3 %all-to-all-done.1 = bf16[32,1,2,520]{3,2,1,0:T(2,128)(2,1)S(1)} async-done(((bf16[32,1,2,520]{3,2,1,0:T(2,128)(2,1)}), bf16[32,1,2,520]{3,2,1,0:T(2,128)(2,1)S(1)}, u32[]{:S(2)}, u32[]{:S(2)}) %all-to-all-start.1) | async-done | bytes 66592 | tf_op jit(solution)/shard_map/all_to_all | solution.py:89
  110.9 0.9 copy-done
  111.8 1.8 %add.219 = f32[2,512,512]{2,1,0:T(8,128)} add(f32[2,512,512]{2,1,0:T(8,128)S(1)} %copy-done, f32[2,512,512]{2,1,0:T(8,128)S(1)} %bitcast.63) | non-fusion elementwise | flops 524288 | bytes 6291456 | tf_op jit(solution)/shard_map/add | solution.py:108
  (65 shorter events, 9.3 us)
Async XLA Ops:
  0.0 11.8 %collective-permute-start = (s32[32,1]{0,1:T(1,128)}, s32[32,1]{0,1:T(1,128)S(1)}, u32[]{:S(2)}, u32[]{:S(2)}) collective-permute-start(s32[32,1]{0,1:T(1,128)} %param.8), channel_id=1, source_target_pairs={{0,2},{2,4},{4,6},{6,8},{8,10},{10,12},{12,14},{14,16},{16,18},{18... | collective-permute-start | bytes 392 | tf_op jit(solution)/shard_map/ppermute | solution.py:63
  2.9 10.5 %collective-permute-start.8 = (s32[32,1]{0,1:T(1,128)}, s32[32,1]{0,1:T(1,128)S(1)}, u32[]{:S(2)}, u32[]{:S(2)}) collective-permute-start(s32[32,1]{0,1:T(1,128)} %param.8), channel_id=1, source_target_pairs={{0,30},{2,0},{4,2},{6,4},{8,6},{10,8},{12,10},{14,12},{16,14},{18,... | collective-permute-start | bytes 392 | tf_op jit(solution)/shard_map/ppermute | solution.py:65
  8.2 30.7 %all-to-all-start = ((bf16[32,1,5]{2,1,0:T(2,128)(2,1)}), bf16[32,1,5]{2,1,0:T(2,128)(2,1)S(1)}, u32[]{:S(2)}, u32[]{:S(2)}) async-start(bf16[32,1,5]{2,1,0:T(2,128)(2,1)} %broadcast_in_dim.21), calls=%async_computation | async-start | bytes 32768 | tf_op jit(solution)/shard_map/all_to_all | solution.py:90
  11.8 7.2 %collective-permute-start.1 = (s32[32,1]{0,1:T(1,128)S(1)}, s32[32,1]{0,1:T(1,128)S(1)}, u32[]{:S(2)}, u32[]{:S(2)}) collective-permute-start(s32[32,1]{0,1:T(1,128)S(1)} %collective-permute-done), channel_id=1, source_target_pairs={{0,2},{2,4},{4,6},{6,8},{8,10},{10,12},{12,14},{14,16},{16,18},{18... | collective-permute-start | bytes 392 | tf_op jit(solution)/shard_map/ppermute | solution.py:63
  13.5 5.5 %collective-permute-start.9 = (s32[32,1]{0,1:T(1,128)S(1)}, s32[32,1]{0,1:T(1,128)S(1)}, u32[]{:S(2)}, u32[]{:S(2)}) collective-permute-start(s32[32,1]{0,1:T(1,128)S(1)} %collective-permute-done.8), channel_id=1, source_target_pairs={{0,30},{2,0},{4,2},{6,4},{8,6},{10,8},{12,10},{14,12},{16,14},{18,... | collective-permute-start | bytes 392 | tf_op jit(solution)/shard_map/ppermute | solution.py:65
  19.0 7.1 %collective-permute-start.2 = (s32[32,1]{0,1:T(1,128)S(1)}, s32[32,1]{0,1:T(1,128)S(1)}, u32[]{:S(2)}, u32[]{:S(2)}) collective-permute-start(s32[32,1]{0,1:T(1,128)S(1)} %collective-permute-done.1), channel_id=1, source_target_pairs={{0,2},{2,4},{4,6},{6,8},{8,10},{10,12},{12,14},{14,16},{16,18},{18... | collective-permute-start | bytes 392 | tf_op jit(solution)/shard_map/ppermute | solution.py:63
  19.0 7.1 %collective-permute-start.10 = (s32[32,1]{0,1:T(1,128)S(1)}, s32[32,1]{0,1:T(1,128)S(1)}, u32[]{:S(2)}, u32[]{:S(2)}) collective-permute-start(s32[32,1]{0,1:T(1,128)S(1)} %collective-permute-done.9), channel_id=1, source_target_pairs={{0,30},{2,0},{4,2},{6,4},{8,6},{10,8},{12,10},{14,12},{16,14},{18,... | collective-permute-start | bytes 392 | tf_op jit(solution)/shard_map/ppermute | solution.py:65
  26.1 7.1 %collective-permute-start.3 = (s32[32,1]{0,1:T(1,128)S(1)}, s32[32,1]{0,1:T(1,128)S(1)}, u32[]{:S(2)}, u32[]{:S(2)}) collective-permute-start(s32[32,1]{0,1:T(1,128)S(1)} %collective-permute-done.2), channel_id=1, source_target_pairs={{0,2},{2,4},{4,6},{6,8},{8,10},{10,12},{12,14},{14,16},{16,18},{18... | collective-permute-start | bytes 392 | tf_op jit(solution)/shard_map/ppermute | solution.py:63
  26.1 7.1 %collective-permute-start.11 = (s32[32,1]{0,1:T(1,128)S(1)}, s32[32,1]{0,1:T(1,128)S(1)}, u32[]{:S(2)}, u32[]{:S(2)}) collective-permute-start(s32[32,1]{0,1:T(1,128)S(1)} %collective-permute-done.10), channel_id=1, source_target_pairs={{0,30},{2,0},{4,2},{6,4},{8,6},{10,8},{12,10},{14,12},{16,14},{18,... | collective-permute-start | bytes 392 | tf_op jit(solution)/shard_map/ppermute | solution.py:65
  33.2 10.1 %collective-permute-start.4 = (s32[32,1]{0,1:T(1,128)S(1)}, s32[32,1]{0,1:T(1,128)S(1)}, u32[]{:S(2)}, u32[]{:S(2)}) collective-permute-start(s32[32,1]{0,1:T(1,128)S(1)} %collective-permute-done.3), channel_id=1, source_target_pairs={{0,2},{2,4},{4,6},{6,8},{8,10},{10,12},{12,14},{14,16},{16,18},{18... | collective-permute-start | bytes 392 | tf_op jit(solution)/shard_map/ppermute | solution.py:63
  33.2 10.1 %collective-permute-start.12 = (s32[32,1]{0,1:T(1,128)S(1)}, s32[32,1]{0,1:T(1,128)S(1)}, u32[]{:S(2)}, u32[]{:S(2)}) collective-permute-start(s32[32,1]{0,1:T(1,128)S(1)} %collective-permute-done.11), channel_id=1, source_target_pairs={{0,30},{2,0},{4,2},{6,4},{8,6},{10,8},{12,10},{14,12},{16,14},{18,... | collective-permute-start | bytes 392 | tf_op jit(solution)/shard_map/ppermute | solution.py:65
  43.3 7.2 %collective-permute-start.5 = (s32[32,1]{0,1:T(1,128)S(1)}, s32[32,1]{0,1:T(1,128)S(1)}, u32[]{:S(2)}, u32[]{:S(2)}) collective-permute-start(s32[32,1]{0,1:T(1,128)S(1)} %collective-permute-done.4), channel_id=1, source_target_pairs={{0,2},{2,4},{4,6},{6,8},{8,10},{10,12},{12,14},{14,16},{16,18},{18... | collective-permute-start | bytes 392 | tf_op jit(solution)/shard_map/ppermute | solution.py:63
  43.4 7.1 %collective-permute-start.13 = (s32[32,1]{0,1:T(1,128)S(1)}, s32[32,1]{0,1:T(1,128)S(1)}, u32[]{:S(2)}, u32[]{:S(2)}) collective-permute-start(s32[32,1]{0,1:T(1,128)S(1)} %collective-permute-done.12), channel_id=1, source_target_pairs={{0,30},{2,0},{4,2},{6,4},{8,6},{10,8},{12,10},{14,12},{16,14},{18,... | collective-permute-start | bytes 392 | tf_op jit(solution)/shard_map/ppermute | solution.py:65
  50.5 7.1 %collective-permute-start.6 = (s32[32,1]{0,1:T(1,128)S(1)}, s32[32,1]{0,1:T(1,128)S(1)}, u32[]{:S(2)}, u32[]{:S(2)}) collective-permute-start(s32[32,1]{0,1:T(1,128)S(1)} %collective-permute-done.5), channel_id=1, source_target_pairs={{0,2},{2,4},{4,6},{6,8},{8,10},{10,12},{12,14},{14,16},{16,18},{18... | collective-permute-start | bytes 392 | tf_op jit(solution)/shard_map/ppermute | solution.py:63
  50.5 7.5 %collective-permute-start.14 = (s32[32,1]{0,1:T(1,128)S(1)}, s32[32,1]{0,1:T(1,128)S(1)}, u32[]{:S(2)}, u32[]{:S(2)}) collective-permute-start(s32[32,1]{0,1:T(1,128)S(1)} %collective-permute-done.13), channel_id=1, source_target_pairs={{0,30},{2,0},{4,2},{6,4},{8,6},{10,8},{12,10},{14,12},{16,14},{18,... | collective-permute-start | bytes 392 | tf_op jit(solution)/shard_map/ppermute | solution.py:65
  57.6 7.1 %collective-permute-start.7 = (s32[32,1]{0,1:T(1,128)S(1)}, s32[32,1]{0,1:T(1,128)S(1)}, u32[]{:S(2)}, u32[]{:S(2)}) collective-permute-start(s32[32,1]{0,1:T(1,128)S(1)} %collective-permute-done.6), channel_id=1, source_target_pairs={{0,2},{2,4},{4,6},{6,8},{8,10},{10,12},{12,14},{14,16},{16,18},{18... | collective-permute-start | bytes 392 | tf_op jit(solution)/shard_map/ppermute | solution.py:63
  99.6 10.2 %all-to-all-start.1 = ((bf16[32,1,2,520]{3,2,1,0:T(2,128)(2,1)}), bf16[32,1,2,520]{3,2,1,0:T(2,128)(2,1)S(1)}, u32[]{:S(2)}, u32[]{:S(2)}) async-start(bf16[32,1,2,520]{3,2,1,0:T(2,128)(2,1)} %fusion.11), calls=%async_computation.1 | async-start | bytes 163840 | tf_op jit(solution)/shard_map/all_to_all | solution.py:89
  110.2 1.6 %copy-start = (f32[2,512,512]{2,1,0:T(8,128)S(1)}, f32[2,512,512]{2,1,0:T(8,128)}, u32[]{:S(2)}) copy-start(f32[2,512,512]{2,1,0:T(8,128)} %param.9) | copy-start | bytes 6291460
